TPU v7x, 512 devices: a whole 4x4x16 slice. The times are simulated.
512 devices in a mesh: param: 32 (over y_lo, z), row: 4 (over x), col: 4 (over y_hi, core).
Axes of the slice: x: 4, y: 4 (y_hi: 2, y_lo: 2; y = y_hi * 2 + y_lo), z: 16, core: 2. Of those that a mesh axis runs over, the one named last changes fastest.
Arguments:
- coefficients: bfloat16 [3, 2, 32, 512], P(None, None, 'row', 'col'), may hold values from -6 to 6
- noise_sigma: float32 [2, 32, 512], P(None, 'row', 'col'), may hold values from 0.5 to 4
- residual: float32 [2, 32, 512], P(None, 'row', 'col'), may hold values from -0.6 to 0.6
- crack_mask: int32 [32, 4], P('row', 'col'), may hold values 0 or 1
- node_panel: bfloat16 [4, 64, 3, 2048], P('row', 'col', None, 'param'), may hold values from -0.41992188 to 0.41992188
Outputs:
- hessian: float32 [2048, 2048], P('param', ('row', 'col'))
- gradient: float32 [2048], P(('param', 'row', 'col'))
All inputs are finite; a program needn't handle non-finite values. No bound on the sum of `crack_mask` on one device may be relied on, other than what follows from the above.
Results may differ from a plain program's by a relative error of at most 0.0055.
Values may be sent and summed in bfloat16 or wider, within the bound.
No kernel may reach another device: no remote copies, remote signals or barrier semaphores. Data moves between devices by JAX's collectives and lax.ppermute only.
A program may use at most 64 MiB of HBM per device.

v0:
```python
import jax
import jax.numpy as jnp
from jax import lax
from jax.sharding import PartitionSpec as P

EL = 8
CAMS = 2
LANES = 128
HIGHEST = lax.Precision.HIGHEST
PARAM_ORDER = (8, 4, 2, 1, 16)
TILE_ORDER = (8, 2, 4, 1)


def corner_shapes(rows, cols):
    vertical = ((jnp.arange(rows) % EL).astype(jnp.float32) + 0.5) / EL
    horizontal = ((jnp.arange(cols) % EL).astype(jnp.float32) + 0.5) / EL
    lower = vertical[:, None]
    right = horizontal[None, :]
    return jnp.stack(
        [(1.0 - lower) * (1.0 - right), (1.0 - lower) * right, lower * (1.0 - right), lower * right]
    )


def doubling_gather(piece, axes, order):
    size = 1
    for bit in order:
        size *= 2
    me = lax.axis_index(axes)
    data = piece[None]
    for bit in order:
        theirs = lax.ppermute(data, axes, [(i, i ^ bit) for i in range(size)])
        data = jnp.concatenate([data, theirs], axis=0)
    wanted = me ^ jnp.arange(size, dtype=jnp.int32)
    position = jnp.zeros((size,), jnp.int32)
    for step, bit in enumerate(order):
        position = position | wanted // bit % 2 << step
    return jnp.take(data, position, axis=0)


def as_lanes(flat, dtype):
    rows = -(-flat.shape[0] // (8 * LANES)) * 8
    flat = jnp.pad(flat.astype(dtype), (0, rows * LANES - flat.shape[0]))
    return flat.reshape(rows, LANES)


def element_corners(nodes):
    extended = jnp.pad(nodes, ((0, 1), (0, 1), (0, 0), (0, 0)))
    corners = jnp.stack(
        [extended[:-1, :-1], extended[:-1, 1:], extended[1:, :-1], extended[1:, 1:]], axis=0
    )
    corners = corners.transpose(0, 3, 1, 2, 4)
    return corners.reshape(12, nodes.shape[0] * nodes.shape[1], nodes.shape[3])


def on_device(coefficients, noise_sigma, residual, crack_mask, node_panel):
    n_param = lax.axis_size("param")
    n_row = lax.axis_size("row")
    n_col = lax.axis_size("col")
    tiles = n_row * n_col
    per_block = n_param // tiles
    rows = noise_sigma.shape[1]
    cols = noise_sigma.shape[2]
    elem_rows = rows // EL
    elem_cols = cols // EL
    node_rows, node_cols, comps, width = node_panel.shape
    elements = elem_rows * elem_cols
    shapes = corner_shapes(rows, cols)
    live_rows = jnp.repeat(crack_mask.astype(jnp.float32), 128, axis=1)
    pixel_scale = live_rows[None] / noise_sigma
    design = (
        shapes[:, None, None] * pixel_scale[None, None] * coefficients.astype(jnp.float32)[None]
    ).astype(jnp.bfloat16)
    design = design.reshape(4, 3, CAMS, elem_rows, EL, elem_cols, EL).transpose(3, 5, 0, 1, 2, 4, 6)
    design = design.reshape(elements, 12, CAMS * EL * EL)
    weighted = (pixel_scale * residual).astype(jnp.bfloat16)
    weighted = weighted.reshape(CAMS, elem_rows, EL, elem_cols, EL).transpose(1, 3, 0, 2, 4)
    weighted = weighted.reshape(elements, CAMS * EL * EL)
    gram = jnp.einsum("eip,ejp->eij", design, design, preferred_element_type=jnp.float32)
    proj = jnp.einsum("eip,ep->ei", design, weighted, preferred_element_type=jnp.float32)
    payload = jnp.concatenate(
        [node_panel.reshape(-1).astype(jnp.float32), gram.reshape(-1), proj.reshape(-1)]
    )
    piece = as_lanes(payload, jnp.float32)
    slots = jnp.zeros((tiles,) + piece.shape, jnp.float32)
    slots = lax.dynamic_update_slice(slots, piece[None], (lax.axis_index(("row", "col")), 0, 0))
    own = lax.psum(slots, ("row", "col"))
    own = own.reshape(tiles, -1)
    n_nodes = node_rows * node_cols * comps * width
    n_gram = elements * 144
    own_nodes = own[:, :n_nodes].reshape(n_row, n_col, node_rows, node_cols, comps, width)
    own_nodes = own_nodes.transpose(0, 2, 1, 3, 4, 5).reshape(
        n_row * node_rows, n_col * node_cols, comps, width
    )
    grams = own[:, n_nodes : n_nodes + n_gram].reshape(n_row, n_col, elem_rows, elem_cols, 12, 12)
    grams = grams.transpose(0, 2, 1, 3, 4, 5).reshape(-1, 12, 12)
    projs = own[:, n_nodes + n_gram : n_nodes + n_gram + elements * 12]
    projs = (
        projs.reshape(n_row, n_col, elem_rows, elem_cols, 12)
        .transpose(0, 2, 1, 3, 4)
        .reshape(-1, 12)
    )
    route = []
    for b in range(n_param):
        for t in range(tiles):
            route.append((b * tiles + t, (per_block * t + b % per_block) * tiles + b // per_block))
    moved = lax.ppermute(
        as_lanes(node_panel.reshape(-1), jnp.bfloat16), ("param", "row", "col"), route
    )
    cross = doubling_gather(moved, "param", PARAM_ORDER).reshape(n_param, -1)[
        :, : node_rows * node_cols * comps * width
    ]
    cross = cross.reshape(n_row, n_col, per_block, node_rows, node_cols, comps, width)
    cross = cross.transpose(0, 3, 1, 4, 5, 2, 6)
    cross = cross.reshape(n_row * node_rows, n_col * node_cols, comps, per_block * width)
    rows_of = element_corners(own_nodes.astype(jnp.bfloat16))
    cols_of = element_corners(cross)
    weighted_rows = jnp.sum(
        grams.transpose(1, 2, 0)[:, :, :, None] * rows_of.astype(jnp.float32)[:, None], axis=0
    )
    high = lax.reduce_precision(weighted_rows, exponent_bits=8, mantissa_bits=7)
    low = weighted_rows - high
    stacked = jnp.concatenate([high.astype(jnp.bfloat16), low.astype(jnp.bfloat16)], axis=2)
    product = jnp.einsum("jep,jeq->pq", stacked, cols_of, preferred_element_type=jnp.float32)
    hessian = product[:width] + product[width:]
    gradient = jnp.einsum("iep,ie->p", rows_of.astype(jnp.float32), projs.T, precision=HIGHEST)
    share = width // tiles
    gradient = lax.dynamic_slice(gradient, (lax.axis_index(("row", "col")) * share,), (share,))
    return (hessian, gradient)


def solution(mesh):
    in_specs = (
        P(None, None, "row", "col"),
        P(None, "row", "col"),
        P(None, "row", "col"),
        P("row", "col"),
        P("row", "col", None, "param"),
    )
    out_specs = (P("param", ("row", "col")), P(("param", "row", "col")))
    return jax.shard_map(
        on_device, mesh=mesh, in_specs=in_specs, out_specs=out_specs, check_vma=False
    )
```

profile of v0, /device:TPU:1, one launch (start us, length us, event | category | flops | bytes accessed | tf_op | source)
XLA Modules:
  0.0 188.7 jit_solution(4385200336250286118)
XLA Ops:
  7.2 0.7 convert_bitcast_fusion
  7.9 0.8 multiply_convert_fusion.1
  8.9 0.9 reshape.641
  11.4 0.9 copy.50
  12.4 6.3 %collective-permute-start = (bf16[24,128]{1,0:T(8,128)(2,1)S(1)}, bf16[24,128]{1,0:T(8,128)(2,1)S(1)}, u32[]{:S(2)}, u32[]{:S(2)}) collective-permute-start(bf16[24,128]{1,0:T(8,128)(2,1)S(1)} %reshape.637), channel_id=1, source_target_pairs={{0,0},{1,32},{2,64},{3,96},{4,128},{5,160},{6,192},{7,224},{8,256}... | collective-permute-start | bytes 18440 | tf_op jit(solution)/shard_map/ppermute | solution.py:106
  18.7 1.2 collective-permute-done
  20.0 21.4 %collective-permute-start.1 = (bf16[1,24,128]{2,1,0:T(8,128)(2,1)S(1)}, bf16[1,24,128]{2,1,0:T(8,128)(2,1)S(1)}, u32[]{:S(2)}, u32[]{:S(2)}) collective-permute-start(bf16[1,24,128]{2,1,0:T(8,128)(2,1)S(1)} %bitcast.74), channel_id=1, source_target_pairs={{0,128},{16,144},{32,160},{48,176},{64,192},{80,208},{96,224},{112... | collective-permute-start | bytes 18440 | tf_op jit(solution)/shard_map/ppermute | solution.py:31
  41.4 1.0 collective-permute-done.1
  42.5 5.2 %collective-permute-start.2 = (bf16[2,24,128]{2,1,0:T(8,128)(2,1)S(1)}, bf16[2,24,128]{2,1,0:T(8,128)(2,1)S(1)}, u32[]{:S(2)}, u32[]{:S(2)}) collective-permute-start(bf16[2,24,128]{2,1,0:T(8,128)(2,1)S(1)} %pad_maximum_fusion.3), channel_id=1, source_target_pairs={{0,64},{16,80},{32,96},{48,112},{64,0},{80,16},{96,32},{112,48},{1... | collective-permute-start | bytes 36872 | tf_op jit(solution)/shard_map/ppermute | solution.py:31
  47.6 3.6 %collective-permute-done.2 = bf16[2,24,128]{2,1,0:T(8,128)(2,1)S(1)} collective-permute-done((bf16[2,24,128]{2,1,0:T(8,128)(2,1)S(1)}, bf16[2,24,128]{2,1,0:T(8,128)(2,1)S(1)}, u32[]{:S(2)}, u32[]{:S(2)}) %collective-permute-start.2) | collective-permute-done | bytes 12320 | tf_op jit(solution)/shard_map/ppermute | solution.py:31
  51.2 3.9 %collective-permute-start.3 = (bf16[4,24,128]{2,1,0:T(8,128)(2,1)S(1)}, bf16[4,24,128]{2,1,0:T(8,128)(2,1)S(1)}, u32[]{:S(2)}, u32[]{:S(2)}) collective-permute-start(bf16[4,24,128]{2,1,0:T(8,128)(2,1)S(1)} %pad_maximum_fusion.2), channel_id=1, source_target_pairs={{0,32},{16,48},{32,0},{48,16},{64,96},{80,112},{96,64},{112,80},{1... | collective-permute-start | bytes 73736 | tf_op jit(solution)/shard_map/ppermute | solution.py:31
  55.1 2.0 %collective-permute-done.3 = bf16[4,24,128]{2,1,0:T(8,128)(2,1)S(1)} collective-permute-done((bf16[4,24,128]{2,1,0:T(8,128)(2,1)S(1)}, bf16[4,24,128]{2,1,0:T(8,128)(2,1)S(1)}, u32[]{:S(2)}, u32[]{:S(2)}) %collective-permute-start.3) | collective-permute-done | bytes 24608 | tf_op jit(solution)/shard_map/ppermute | solution.py:31
  57.1 2.6 %collective-permute-start.4 = (bf16[8,24,128]{2,1,0:T(8,128)(2,1)S(1)}, bf16[8,24,128]{2,1,0:T(8,128)(2,1)S(1)}, u32[]{:S(2)}, u32[]{:S(2)}) collective-permute-start(bf16[8,24,128]{2,1,0:T(8,128)(2,1)S(1)} %pad_maximum_fusion.1), channel_id=1, source_target_pairs={{0,16},{16,0},{32,48},{48,32},{64,80},{80,64},{96,112},{112,96},{1... | collective-permute-start | bytes 147464 | tf_op jit(solution)/shard_map/ppermute | solution.py:31
  59.7 2.5 %collective-permute-done.4 = bf16[8,24,128]{2,1,0:T(8,128)(2,1)S(1)} collective-permute-done((bf16[8,24,128]{2,1,0:T(8,128)(2,1)S(1)}, bf16[8,24,128]{2,1,0:T(8,128)(2,1)S(1)}, u32[]{:S(2)}, u32[]{:S(2)}) %collective-permute-start.4) | collective-permute-done | bytes 49184 | tf_op jit(solution)/shard_map/ppermute | solution.py:31
  62.2 5.1 %collective-permute-start.5 = (bf16[16,24,128]{2,1,0:T(8,128)(2,1)S(1)}, bf16[16,24,128]{2,1,0:T(8,128)(2,1)S(1)}, u32[]{:S(2)}, u32[]{:S(2)}) collective-permute-start(bf16[16,24,128]{2,1,0:T(8,128)(2,1)S(1)} %get-tuple-element.12), channel_id=1, source_target_pairs={{0,256},{16,272},{32,288},{48,304},{64,320},{80,336},{96,352},{112... | collective-permute-start | bytes 294920 | tf_op jit(solution)/shard_map/ppermute | solution.py:31
  67.4 2.0 %collective-permute-done.5 = bf16[16,24,128]{2,1,0:T(8,128)(2,1)S(1)} collective-permute-done((bf16[16,24,128]{2,1,0:T(8,128)(2,1)S(1)}, bf16[16,24,128]{2,1,0:T(8,128)(2,1)S(1)}, u32[]{:S(2)}, u32[]{:S(2)}) %collective-permute-start.5) | collective-permute-done | bytes 98336 | tf_op jit(solution)/shard_map/ppermute | solution.py:31
  69.4 0.6 gather_fusion
  70.3 0.3 select_bitcast_fusion
  70.6 0.5 copy.42
  71.7 0.9 copy.44
  72.7 99.9 %all-reduce.5.cloned.1.call-done = f32[16,6144]{1,0:T(8,128)} async-done(((f32[16,6144]{1,0:T(8,128)}), f32[16,6144]{1,0:T(8,128)}) %all-reduce.5.cloned.1.call-update) | async-done | bytes 393232 | tf_op jit(solution)/shard_map/psum | solution.py:86
  172.5 0.9 slice.68
  174.2 1.1 maximum_bitcast_fusion
  175.2 0.9 copy.40
  176.2 0.5 reshape.636
  176.9 0.4 convolution_bitcast_fusion.1
  177.3 1.0 reshape_transpose_reshape.7
  178.3 0.8 copy.39
  179.2 0.7 multiply_reduce_fusion
  180.3 0.4 convolution_bitcast_fusion
  180.7 0.6 slice_add_fusion
  181.3 0.6 dynamic_slice.3
  (57 shorter events, 4.3 us)
Async XLA Ops:
  7.2 165.4 %all-reduce.5.cloned.1.call-start = ((), (), s32[]{:S(2)}) async-start(), calls=%async_computation | async-start | bytes 786432 | tf_op jit(solution)/shard_map/psum | solution.py:86
  8.7 2.6 %copy-start.1 = (bf16[1,16,3,64]{3,1,2,0:T(8,128)(2,1)S(1)}, bf16[1,16,3,64]{3,1,2,0:T(8,128)(2,1)}, u32[]{:S(2)}) copy-start(bf16[1,16,3,64]{3,1,2,0:T(8,128)(2,1)} %param.9) | copy-start | bytes 18436
  12.4 7.6 %collective-permute-start = (bf16[24,128]{1,0:T(8,128)(2,1)S(1)}, bf16[24,128]{1,0:T(8,128)(2,1)S(1)}, u32[]{:S(2)}, u32[]{:S(2)}) collective-permute-start(bf16[24,128]{1,0:T(8,128)(2,1)S(1)} %reshape.637), channel_id=1, source_target_pairs={{0,0},{1,32},{2,64},{3,96},{4,128},{5,160},{6,192},{7,224},{8,256}... | collective-permute-start | bytes 18440 | tf_op jit(solution)/shard_map/ppermute | solution.py:106
  20.0 22.5 %collective-permute-start.1 = (bf16[1,24,128]{2,1,0:T(8,128)(2,1)S(1)}, bf16[1,24,128]{2,1,0:T(8,128)(2,1)S(1)}, u32[]{:S(2)}, u32[]{:S(2)}) collective-permute-start(bf16[1,24,128]{2,1,0:T(8,128)(2,1)S(1)} %bitcast.74), channel_id=1, source_target_pairs={{0,128},{16,144},{32,160},{48,176},{64,192},{80,208},{96,224},{112... | collective-permute-start | bytes 18440 | tf_op jit(solution)/shard_map/ppermute | solution.py:31
  42.5 8.7 %collective-permute-start.2 = (bf16[2,24,128]{2,1,0:T(8,128)(2,1)S(1)}, bf16[2,24,128]{2,1,0:T(8,128)(2,1)S(1)}, u32[]{:S(2)}, u32[]{:S(2)}) collective-permute-start(bf16[2,24,128]{2,1,0:T(8,128)(2,1)S(1)} %pad_maximum_fusion.3), channel_id=1, source_target_pairs={{0,64},{16,80},{32,96},{48,112},{64,0},{80,16},{96,32},{112,48},{1... | collective-permute-start | bytes 36872 | tf_op jit(solution)/shard_map/ppermute | solution.py:31
  51.2 5.9 %collective-permute-start.3 = (bf16[4,24,128]{2,1,0:T(8,128)(2,1)S(1)}, bf16[4,24,128]{2,1,0:T(8,128)(2,1)S(1)}, u32[]{:S(2)}, u32[]{:S(2)}) collective-permute-start(bf16[4,24,128]{2,1,0:T(8,128)(2,1)S(1)} %pad_maximum_fusion.2), channel_id=1, source_target_pairs={{0,32},{16,48},{32,0},{48,16},{64,96},{80,112},{96,64},{112,80},{1... | collective-permute-start | bytes 73736 | tf_op jit(solution)/shard_map/ppermute | solution.py:31
  57.1 5.1 %collective-permute-start.4 = (bf16[8,24,128]{2,1,0:T(8,128)(2,1)S(1)}, bf16[8,24,128]{2,1,0:T(8,128)(2,1)S(1)}, u32[]{:S(2)}, u32[]{:S(2)}) collective-permute-start(bf16[8,24,128]{2,1,0:T(8,128)(2,1)S(1)} %pad_maximum_fusion.1), channel_id=1, source_target_pairs={{0,16},{16,0},{32,48},{48,32},{64,80},{80,64},{96,112},{112,96},{1... | collective-permute-start | bytes 147464 | tf_op jit(solution)/shard_map/ppermute | solution.py:31
  62.2 7.2 %collective-permute-start.5 = (bf16[16,24,128]{2,1,0:T(8,128)(2,1)S(1)}, bf16[16,24,128]{2,1,0:T(8,128)(2,1)S(1)}, u32[]{:S(2)}, u32[]{:S(2)}) collective-permute-start(bf16[16,24,128]{2,1,0:T(8,128)(2,1)S(1)} %get-tuple-element.12), channel_id=1, source_target_pairs={{0,256},{16,272},{32,288},{48,304},{64,320},{80,336},{96,352},{112... | collective-permute-start | bytes 294920 | tf_op jit(solution)/shard_map/ppermute | solution.py:31
  174.2 2.5 %slice-start = ((f32[16,6144]{1,0:T(8,128)}), f32[16,192]{1,0:T(8,128)S(1)}, s32[]{:S(2)}) async-start(f32[16,6144]{1,0:T(8,128)} %all-reduce.5.cloned.1.call-done), calls=%async_computation.1 | async-start | bytes 32768 | tf_op jit(solution)/shard_map/slice | solution.py:96
  176.2 1.2 slice-start.1
  179.2 1.1 copy-start
Sparse Core Ops, SparseCore 0:
  12.4 160.0 all-reduce.4
where the time goes:
time: 189 us
  waiting for transfers between devices  112 us (59%)
  starting transfers between devices  44.5 us (24%)
  between operations  14.4 us (8%)
  local copies, waits for them, and re-layouts  11.7 us (6%)
  other arithmetic  4.86 us (3%)
    psum x1, waiting for transfers between devices, on_device(): own = lax.psum(slots, ('row', 'col'))  99.9 us
    ppermute x5, starting transfers between devices, doubling_gather(): theirs = lax.ppermute(data, axes, [(i, i ^ bit) for i in range(size)])  38.1 us
    ppermute x5, waiting for transfers between devices, doubling_gather(): theirs = lax.ppermute(data, axes, [(i, i ^ bit) for i in range(size)])  11 us
    ppermute x1, starting transfers between devices, on_device(): lax.ppermute(as_lanes(node_panel.reshape(-1), jnp.bfloat16), ('param', 'r...  6.27 us
  transfers between devices with their start and end apart: 7, of which 7 were waited for; matrix products, arithmetic and copies ran while one was open for 2% of the time, Pallas kernels for 0%

commit v1 on v0

--- a/solution.py
+++ b/solution.py
@@ -83,7 +83,7 @@
     piece = as_lanes(payload, jnp.float32)
     slots = jnp.zeros((tiles,) + piece.shape, jnp.float32)
     slots = lax.dynamic_update_slice(slots, piece[None], (lax.axis_index(("row", "col")), 0, 0))
-    own = lax.psum(slots, ("row", "col"))
+    own = jnp.sum(lax.all_gather(slots, ("row", "col")), axis=0)
     own = own.reshape(tiles, -1)
     n_nodes = node_rows * node_cols * comps * width
     n_gram = elements * 144

time: 189 us -> 120 us (0.63)
  waiting for transfers between devices: 112 us -> 37.7 us
  other arithmetic: 4.86 us -> 8.03 us
    psum x1 -> x0, waiting for transfers between devices: 99.9 us -> none  [on_device(): own = lax.psum(slots, ('row', 'col'))]
    all_gather x0 -> x1, waiting for transfers between devices: none -> 24.7 us  [on_device(): own = jnp.sum(lax.all_gather(slots, ('row', 'col')), axis=0)]
    reduce_sum x0 -> x1, other arithmetic: none -> 3.16 us  [on_device(): own = jnp.sum(lax.all_gather(slots, ('row', 'col')), axis=0)]
  transfers between devices with their start and end apart: 7 -> 7, of which waited for: 7 -> 7; matrix products, arithmetic and copies ran while one was open for 2% -> 4% of each run, Pallas kernels for 0% -> 0%
where the time goes in v1:
time: 120 us; the launch traced here: 119 us
  starting transfers between devices  45.1 us (38%)
  waiting for transfers between devices  37.7 us (31%)
  between operations  14.4 us (12%)
  local copies, waits for them, and re-layouts  12 us (10%)
  other arithmetic  8.03 us (7%)
  matrix products  2.2 us (2%)
    ppermute x5, starting transfers between devices, doubling_gather(): theirs = lax.ppermute(data, axes, [(i, i ^ bit) for i in range(size)])  38.8 us
    all_gather x1, waiting for transfers between devices, on_device(): own = jnp.sum(lax.all_gather(slots, ('row', 'col')), axis=0)  24.7 us
    ppermute x5, waiting for transfers between devices, doubling_gather(): theirs = lax.ppermute(data, axes, [(i, i ^ bit) for i in range(size)])  11.7 us
    ppermute x1, starting transfers between devices, on_device(): lax.ppermute(as_lanes(node_panel.reshape(-1), jnp.bfloat16), ('param', 'r...  6.27 us
    reduce_sum x1, other arithmetic, on_device(): own = jnp.sum(lax.all_gather(slots, ('row', 'col')), axis=0)  3.16 us
  transfers between devices with their start and end apart: 7, of which 7 were waited for; matrix products, arithmetic and copies ran while one was open for 4% of the time, Pallas kernels for 0%

profile of v1, /device:TPU:1, one launch (start us, length us, event | category | flops | bytes accessed | tf_op | source)
XLA Modules:
  0.0 119.4 jit_solution(16542863900909760636)
XLA Ops:
  7.2 0.7 convert_bitcast_fusion
  7.9 0.8 multiply_convert_fusion.1
  8.9 0.9 reshape.644
  11.3 0.7 copy.46
  12.1 0.7 copy-done
  12.9 0.7 copy.54
  13.7 6.3 %collective-permute-start = (bf16[24,128]{1,0:T(8,128)(2,1)S(1)}, bf16[24,128]{1,0:T(8,128)(2,1)S(1)}, u32[]{:S(2)}, u32[]{:S(2)}) collective-permute-start(bf16[24,128]{1,0:T(8,128)(2,1)S(1)} %reshape.640), channel_id=1, source_target_pairs={{0,0},{1,32},{2,64},{3,96},{4,128},{5,160},{6,192},{7,224},{8,256}... | collective-permute-start | bytes 18440 | tf_op jit(solution)/shard_map/ppermute | solution.py:106
  20.0 1.2 %collective-permute-done = bf16[24,128]{1,0:T(8,128)(2,1)S(1)} collective-permute-done((bf16[24,128]{1,0:T(8,128)(2,1)S(1)}, bf16[24,128]{1,0:T(8,128)(2,1)S(1)}, u32[]{:S(2)}, u32[]{:S(2)}) %collective-permute-start) | collective-permute-done | bytes 6176 | tf_op jit(solution)/shard_map/ppermute | solution.py:106
  21.3 21.4 %collective-permute-start.1 = (bf16[1,24,128]{2,1,0:T(8,128)(2,1)S(1)}, bf16[1,24,128]{2,1,0:T(8,128)(2,1)S(1)}, u32[]{:S(2)}, u32[]{:S(2)}) collective-permute-start(bf16[1,24,128]{2,1,0:T(8,128)(2,1)S(1)} %bitcast.76), channel_id=1, source_target_pairs={{0,128},{16,144},{32,160},{48,176},{64,192},{80,208},{96,224},{112... | collective-permute-start | bytes 18440 | tf_op jit(solution)/shard_map/ppermute | solution.py:31
  42.7 1.0 collective-permute-done.1
  43.7 5.2 %collective-permute-start.2 = (bf16[2,24,128]{2,1,0:T(8,128)(2,1)S(1)}, bf16[2,24,128]{2,1,0:T(8,128)(2,1)S(1)}, u32[]{:S(2)}, u32[]{:S(2)}) collective-permute-start(bf16[2,24,128]{2,1,0:T(8,128)(2,1)S(1)} %pad_maximum_fusion.3), channel_id=1, source_target_pairs={{0,64},{16,80},{32,96},{48,112},{64,0},{80,16},{96,32},{112,48},{1... | collective-permute-start | bytes 36872 | tf_op jit(solution)/shard_map/ppermute | solution.py:31
  48.9 3.2 %collective-permute-done.2 = bf16[2,24,128]{2,1,0:T(8,128)(2,1)S(1)} collective-permute-done((bf16[2,24,128]{2,1,0:T(8,128)(2,1)S(1)}, bf16[2,24,128]{2,1,0:T(8,128)(2,1)S(1)}, u32[]{:S(2)}, u32[]{:S(2)}) %collective-permute-start.2) | collective-permute-done | bytes 12320 | tf_op jit(solution)/shard_map/ppermute | solution.py:31
  52.1 4.3 %collective-permute-start.3 = (bf16[4,24,128]{2,1,0:T(8,128)(2,1)S(1)}, bf16[4,24,128]{2,1,0:T(8,128)(2,1)S(1)}, u32[]{:S(2)}, u32[]{:S(2)}) collective-permute-start(bf16[4,24,128]{2,1,0:T(8,128)(2,1)S(1)} %pad_maximum_fusion.2), channel_id=1, source_target_pairs={{0,32},{16,48},{32,0},{48,16},{64,96},{80,112},{96,64},{112,80},{1... | collective-permute-start | bytes 73736 | tf_op jit(solution)/shard_map/ppermute | solution.py:31
  56.4 1.2 collective-permute-done.3
  57.6 2.6 %collective-permute-start.4 = (bf16[8,24,128]{2,1,0:T(8,128)(2,1)S(1)}, bf16[8,24,128]{2,1,0:T(8,128)(2,1)S(1)}, u32[]{:S(2)}, u32[]{:S(2)}) collective-permute-start(bf16[8,24,128]{2,1,0:T(8,128)(2,1)S(1)} %pad_maximum_fusion.1), channel_id=1, source_target_pairs={{0,16},{16,0},{32,48},{48,32},{64,80},{80,64},{96,112},{112,96},{1... | collective-permute-start | bytes 147464 | tf_op jit(solution)/shard_map/ppermute | solution.py:31
  60.3 2.2 %collective-permute-done.4 = bf16[8,24,128]{2,1,0:T(8,128)(2,1)S(1)} collective-permute-done((bf16[8,24,128]{2,1,0:T(8,128)(2,1)S(1)}, bf16[8,24,128]{2,1,0:T(8,128)(2,1)S(1)}, u32[]{:S(2)}, u32[]{:S(2)}) %collective-permute-start.4) | collective-permute-done | bytes 49184 | tf_op jit(solution)/shard_map/ppermute | solution.py:31
  62.4 5.3 %collective-permute-start.5 = (bf16[16,24,128]{2,1,0:T(8,128)(2,1)S(1)}, bf16[16,24,128]{2,1,0:T(8,128)(2,1)S(1)}, u32[]{:S(2)}, u32[]{:S(2)}) collective-permute-start(bf16[16,24,128]{2,1,0:T(8,128)(2,1)S(1)} %get-tuple-element.12), channel_id=1, source_target_pairs={{0,256},{16,272},{32,288},{48,304},{64,320},{80,336},{96,352},{112... | collective-permute-start | bytes 294920 | tf_op jit(solution)/shard_map/ppermute | solution.py:31
  67.8 4.2 %collective-permute-done.5 = bf16[16,24,128]{2,1,0:T(8,128)(2,1)S(1)} collective-permute-done((bf16[16,24,128]{2,1,0:T(8,128)(2,1)S(1)}, bf16[16,24,128]{2,1,0:T(8,128)(2,1)S(1)}, u32[]{:S(2)}, u32[]{:S(2)}) %collective-permute-start.5) | collective-permute-done | bytes 98336 | tf_op jit(solution)/shard_map/ppermute | solution.py:31
  72.1 0.6 gather_fusion
  73.3 0.5 copy.55
  74.4 1.0 copy.57
  75.4 24.7 %all-gather.2.cloned.1.call-done = f32[16,16,48,128]{3,2,1,0:T(8,128)} async-done(((f32[1,16,48,128]{3,2,1,0:T(8,128)}), f32[16,16,48,128]{3,2,1,0:T(8,128)}) %all-gather.2.cloned.1.call-update) | async-done | bytes 6291472 | tf_op jit(solution)/shard_map/all_gather | solution.py:86
  100.0 3.2 %reduce_sum.18 = f32[16,48,128]{2,1,0:T(8,128)S(1)} reduce(f32[16,16,48,128]{3,2,1,0:T(8,128)} %all-gather.2.cloned.1.call-done, f32[]{:T(128)} %constant.156.clone.1), dimensions={0}, to_apply=%region_0.1 | reduce | flops 1474560 | bytes 6684676 | tf_op jit(solution)/shard_map/reduce_sum | solution.py:86
  104.1 1.1 maximum_bitcast_fusion
  105.1 0.9 copy.53
  106.0 0.5 reshape.639
  107.2 1.0 reshape_transpose_reshape.7
  108.2 0.8 copy.52
  109.0 0.7 multiply_reduce_fusion
  109.9 1.5 %convolution_bitcast_fusion = f32[128,128]{1,0:T(8,128)S(1)} fusion(bf16[12,256,128]{2,1,0:T(8,128)(2,1)} %bitcast.72, bf16[12,256,64]{1,2,0:T(8,128)(2,1)S(1)} %get-tuple-element.5, bf16[12,256,64]{1,2,0:T(8,128)(2,1)S(1)} %get-tuple-element.4), kind=kOutput, calls=%fused_computation.4 | convolution fusion | flops 102236160 | bytes 1638400 | tf_op jit(solution)/shard_map/jep,jeq->pq/dot_general | solution.py:123
  111.4 0.6 slice_add_fusion
  112.0 0.6 dynamic_slice.3
  (54 shorter events, 4.8 us)
Async XLA Ops:
  7.2 92.9 %all-gather.2.cloned.1.call-start = ((), (), s32[]{:S(2)}) async-start(), calls=%async_computation | async-start | bytes 6684672 | tf_op jit(solution)/shard_map/all_gather | solution.py:86
  12.1 0.7 copy-start
  13.7 7.6 %collective-permute-start = (bf16[24,128]{1,0:T(8,128)(2,1)S(1)}, bf16[24,128]{1,0:T(8,128)(2,1)S(1)}, u32[]{:S(2)}, u32[]{:S(2)}) collective-permute-start(bf16[24,128]{1,0:T(8,128)(2,1)S(1)} %reshape.640), channel_id=1, source_target_pairs={{0,0},{1,32},{2,64},{3,96},{4,128},{5,160},{6,192},{7,224},{8,256}... | collective-permute-start | bytes 18440 | tf_op jit(solution)/shard_map/ppermute | solution.py:106
  21.3 22.5 %collective-permute-start.1 = (bf16[1,24,128]{2,1,0:T(8,128)(2,1)S(1)}, bf16[1,24,128]{2,1,0:T(8,128)(2,1)S(1)}, u32[]{:S(2)}, u32[]{:S(2)}) collective-permute-start(bf16[1,24,128]{2,1,0:T(8,128)(2,1)S(1)} %bitcast.76), channel_id=1, source_target_pairs={{0,128},{16,144},{32,160},{48,176},{64,192},{80,208},{96,224},{112... | collective-permute-start | bytes 18440 | tf_op jit(solution)/shard_map/ppermute | solution.py:31
  43.7 8.3 %collective-permute-start.2 = (bf16[2,24,128]{2,1,0:T(8,128)(2,1)S(1)}, bf16[2,24,128]{2,1,0:T(8,128)(2,1)S(1)}, u32[]{:S(2)}, u32[]{:S(2)}) collective-permute-start(bf16[2,24,128]{2,1,0:T(8,128)(2,1)S(1)} %pad_maximum_fusion.3), channel_id=1, source_target_pairs={{0,64},{16,80},{32,96},{48,112},{64,0},{80,16},{96,32},{112,48},{1... | collective-permute-start | bytes 36872 | tf_op jit(solution)/shard_map/ppermute | solution.py:31
  52.1 5.5 %collective-permute-start.3 = (bf16[4,24,128]{2,1,0:T(8,128)(2,1)S(1)}, bf16[4,24,128]{2,1,0:T(8,128)(2,1)S(1)}, u32[]{:S(2)}, u32[]{:S(2)}) collective-permute-start(bf16[4,24,128]{2,1,0:T(8,128)(2,1)S(1)} %pad_maximum_fusion.2), channel_id=1, source_target_pairs={{0,32},{16,48},{32,0},{48,16},{64,96},{80,112},{96,64},{112,80},{1... | collective-permute-start | bytes 73736 | tf_op jit(solution)/shard_map/ppermute | solution.py:31
  57.6 4.8 %collective-permute-start.4 = (bf16[8,24,128]{2,1,0:T(8,128)(2,1)S(1)}, bf16[8,24,128]{2,1,0:T(8,128)(2,1)S(1)}, u32[]{:S(2)}, u32[]{:S(2)}) collective-permute-start(bf16[8,24,128]{2,1,0:T(8,128)(2,1)S(1)} %pad_maximum_fusion.1), channel_id=1, source_target_pairs={{0,16},{16,0},{32,48},{48,32},{64,80},{80,64},{96,112},{112,96},{1... | collective-permute-start | bytes 147464 | tf_op jit(solution)/shard_map/ppermute | solution.py:31
  62.4 9.6 %collective-permute-start.5 = (bf16[16,24,128]{2,1,0:T(8,128)(2,1)S(1)}, bf16[16,24,128]{2,1,0:T(8,128)(2,1)S(1)}, u32[]{:S(2)}, u32[]{:S(2)}) collective-permute-start(bf16[16,24,128]{2,1,0:T(8,128)(2,1)S(1)} %get-tuple-element.12), channel_id=1, source_target_pairs={{0,256},{16,272},{32,288},{48,304},{64,320},{80,336},{96,352},{112... | collective-permute-start | bytes 294920 | tf_op jit(solution)/shard_map/ppermute | solution.py:31
Sparse Core Ops, SparseCore 0:
  13.0 86.9 all-gather.1
